TPU v7x, 32 devices: a whole 2x2x4 slice. The times are simulated.
32 devices in a mesh: dp: 4 (over z), tensor: 8 (over y, x, core).
Axes of the slice: x: 2, y: 2, z: 4, core: 2. Of those that a mesh axis runs over, the one named last changes fastest.
Arguments:
- inputs: bfloat16 [4, 32, 4096], P(None, 'tensor', 'dp'), may hold values from -6 to 6
- norm_gain: float32 [4096], P('dp'), may hold values from 0.1 to 1.9
- w_gate: bfloat16 [4096, 28672], P('dp', 'tensor'), may hold values from -0.09375 to 0.09375
- w_up: bfloat16 [4096, 28672], P('dp', 'tensor'), may hold values from -0.09375 to 0.09375
- w_down: bfloat16 [28672, 4096], P('tensor', 'dp'), may hold values from -0.03125 to 0.03125
- d_output: bfloat16 [4, 32, 4096], P(None, 'tensor', 'dp'), may hold values from -0.75 to 0.75
- level_of_batch: int32 [4], replicated, may hold values from 0 to 3, each once
Outputs:
- outputs: bfloat16 [4, 32, 4096], P(None, 'tensor', 'dp')
- d_inputs: bfloat16 [4, 32, 4096], P(None, 'tensor', 'dp')
- d_gain: float32 [4096], P('dp')
- d_gate: bfloat16 [4096, 28672], P('dp', 'tensor')
- d_up: bfloat16 [4096, 28672], P('dp', 'tensor')
- d_down: bfloat16 [28672, 4096], P('tensor', 'dp')
- row_product: float32 [4, 32], P(None, 'tensor')
Inputs may be any that keep to these rules, and one draw needn't show every extreme that they name: `level_of_batch`: every level from 0 to 3 belongs to exactly one micro-batch.
All inputs are finite; a program needn't handle non-finite values.
Results may differ from a plain program's by a relative error of at most 0.02.
Values may be sent and summed in bfloat16 or wider, within the bound.
No kernel may reach another device: no remote copies, remote signals or barrier semaphores. Data moves between devices by JAX's collectives and lax.ppermute only.
A program may use at most 384 MiB of HBM per device.

v0:
```python
import jax
import jax.numpy as jnp
from jax import lax
from jax.sharding import PartitionSpec as P

epsilon = 1e-05
contract_cols = (((1,), (1,)), ((), ()))
contract_rows = (((0,), (0,)), ((), ()))


def local_terms(gate_sum, up_sum, back_sum, active_mask):
    sigmoid_gate = jax.nn.sigmoid(gate_sum)
    silu_gate = gate_sum * sigmoid_gate
    slope = sigmoid_gate * (1.0 + gate_sum * (1.0 - sigmoid_gate))
    hidden = (silu_gate * up_sum * active_mask).astype(jnp.bfloat16)
    gate_grad = (back_sum * up_sum * slope * active_mask).astype(jnp.bfloat16)
    up_grad = (back_sum * silu_gate * active_mask).astype(jnp.bfloat16)
    return (hidden, gate_grad, up_grad)


def per_device(inputs, norm_gain, w_gate, w_up, w_down, d_output, level_of_batch):
    groups = lax.axis_size("tensor")
    tensor_index = lax.axis_index("tensor")
    local_feat = w_gate.shape[0]
    local_cols = w_gate.shape[1]
    full_width = local_feat * lax.axis_size("dp")
    batches, local_rows, _ = inputs.shape
    wide_inputs = inputs.astype(jnp.float32)
    grad_all = lax.all_gather(d_output.transpose(1, 0, 2), "tensor", axis=0, tiled=True)
    rows = grad_all.shape[0]
    start = tensor_index * local_rows
    flat_grad = grad_all.reshape(rows * batches, local_feat)
    back_part = lax.dot_general(
        flat_grad, w_down, contract_cols, preferred_element_type=jnp.float32
    ).astype(jnp.bfloat16)
    back_first = lax.psum(back_part, "dp")
    inputs_all, _ = lax.optimization_barrier((inputs.transpose(1, 0, 2), back_part))
    inputs_all = lax.all_gather(inputs_all, "tensor", axis=0, tiled=True).astype(jnp.float32)
    square_sum = lax.psum(jnp.sum(inputs_all * inputs_all, axis=2).T, "dp").T
    row_scale_all = lax.rsqrt(square_sum / full_width + epsilon)
    normed_all = (inputs_all * row_scale_all[:, :, None] * norm_gain).astype(jnp.bfloat16)
    row_scale = lax.dynamic_slice_in_dim(row_scale_all, start, local_rows, axis=0).T
    flat_normed = normed_all.reshape(rows * batches, local_feat)
    halvings = 3 - level_of_batch
    active = (tensor_index < jnp.right_shift(groups, halvings)).astype(jnp.float32)
    active_mask = jnp.tile(active, rows)[:, None]
    chunks = 1
    width = local_cols // chunks
    down_part = None
    normed_part = None
    hiddens, gate_grads, up_grads = ([], [], [])
    for chunk in range(chunks):
        cols = slice(chunk * width, (chunk + 1) * width)
        gate_w = w_gate[:, cols]
        up_w = w_up[:, cols]
        down_w = w_down[cols, :]
        gate_part = jnp.dot(flat_normed, gate_w, preferred_element_type=jnp.float32)
        up_part = jnp.dot(flat_normed, up_w, preferred_element_type=jnp.float32)
        parts = (gate_part.astype(jnp.bfloat16), up_part.astype(jnp.bfloat16))
        parts, back_sum = lax.optimization_barrier((parts, back_first))
        gate_sum, up_sum = lax.psum(parts, "dp")
        hidden, gate_grad, up_grad = local_terms(
            gate_sum.astype(jnp.float32),
            up_sum.astype(jnp.float32),
            back_sum.astype(jnp.float32),
            active_mask,
        )
        hiddens.append(hidden)
        gate_grads.append(gate_grad)
        up_grads.append(up_grad)
        down_term = jnp.dot(hidden, down_w, preferred_element_type=jnp.float32)
        normed_term = lax.dot_general(
            gate_grad, gate_w, contract_cols, preferred_element_type=jnp.float32
        ) + lax.dot_general(up_grad, up_w, contract_cols, preferred_element_type=jnp.float32)
        down_part = down_term if down_part is None else down_part + down_term
        normed_part = normed_term if normed_part is None else normed_part + normed_term
    hidden = jnp.concatenate(hiddens, axis=1)
    gate_grad = jnp.concatenate(gate_grads, axis=1)
    up_grad = jnp.concatenate(up_grads, axis=1)
    stacked = jnp.stack(
        [
            down_part.reshape(rows, batches, local_feat),
            normed_part.reshape(rows, batches, local_feat),
        ],
        axis=1,
    ).astype(jnp.bfloat16)
    stacked = stacked.reshape(rows, 2 * batches, local_feat)
    scaled_all = (inputs_all * row_scale_all[:, :, None]).reshape(rows * batches, local_feat)
    gain_part = jnp.sum(normed_part * scaled_all, axis=0)
    row_all = jnp.sum(
        normed_part * (norm_gain * inputs_all.reshape(rows * batches, local_feat)), axis=1
    )
    reduced = lax.psum(jnp.concatenate([gain_part, row_all]), "tensor")
    d_gain = reduced[:local_feat]
    row_all = lax.psum(reduced[local_feat:], "dp").reshape(rows, batches)
    row_product = lax.dynamic_slice_in_dim(row_all, start, local_rows, axis=0).T
    hidden, flat_grad, _ = lax.optimization_barrier((hidden, flat_grad, stacked))
    shares = lax.psum_scatter(stacked, "tensor", scatter_dimension=0, tiled=True).astype(
        jnp.float32
    )
    shares = shares.reshape(local_rows, 2, batches, local_feat)
    down_output = shares[:, 0].transpose(1, 0, 2)
    normed_grad = shares[:, 1].transpose(1, 0, 2)
    down_out = lax.dot_general(
        hidden, flat_grad, contract_rows, preferred_element_type=jnp.float32
    ).astype(jnp.bfloat16)
    gate_out = lax.dot_general(
        flat_normed, gate_grad, contract_rows, preferred_element_type=jnp.float32
    ).astype(jnp.bfloat16)
    up_out = lax.dot_general(
        flat_normed, up_grad, contract_rows, preferred_element_type=jnp.float32
    ).astype(jnp.bfloat16)
    wide_grad = d_output.astype(jnp.float32)
    weighted = norm_gain * normed_grad
    outputs = (wide_inputs + down_output).astype(jnp.bfloat16)
    scale_cube = row_scale * row_scale * row_scale
    d_inputs = (
        wide_grad
        + row_scale[:, :, None] * weighted
        - wide_inputs * (scale_cube * row_product / full_width)[:, :, None]
    ).astype(jnp.bfloat16)
    return (outputs, d_inputs, d_gain, gate_out, up_out, down_out, row_product)


def solution(mesh):
    in_specs = (
        P(None, "tensor", "dp"),
        P("dp"),
        P("dp", "tensor"),
        P("dp", "tensor"),
        P("tensor", "dp"),
        P(None, "tensor", "dp"),
        P(),
    )
    out_specs = (
        P(None, "tensor", "dp"),
        P(None, "tensor", "dp"),
        P("dp"),
        P("dp", "tensor"),
        P("dp", "tensor"),
        P("tensor", "dp"),
        P(None, "tensor"),
    )
    return jax.shard_map(
        per_device, mesh=mesh, in_specs=in_specs, out_specs=out_specs, check_vma=False
    )
```

profile of v0, /device:TPU:0, one launch (start us, length us, event | category | flops | bytes accessed | tf_op | source)
XLA Modules:
  0.0 222.1 jit_solution(7097210431955141305)
XLA Ops:
  7.2 0.0 all-reduce.4.cloned.1.call-start
  7.2 0.8 copy.45
  8.0 0.8 copy.44
  8.8 10.8 %all_gather.6 = bf16[32,4,1024]{2,1,0:T(4,128)(2,1)S(1)} all-gather(bf16[4,4,1024]{2,1,0:T(4,128)(2,1)S(1)} %bitcast.61), channel_id=1, replica_groups=mesh['dp'=4,'tensor'=8] {'tensor'}, dimensions={0}, use_global_device_ids=true | all-gather | bytes 294912 | tf_op jit(solution)/shard_map/all_gather | solution.py:29
  19.6 0.1 reshape.45
  19.6 6.6 %convolution_convert_fusion.5 = bf16[128,3584]{1,0:T(8,128)(2,1)} fusion(bf16[128,1024]{1,0:T(8,128)(2,1)S(1)} %reshape.45, bf16[3584,1024]{1,0:T(8,128)(2,1)} %param.11), kind=kOutput, calls=%fused_computation.5 | convolution fusion | flops 939982848 | bytes 8519680 | tf_op jit(solution)/shard_map/dot_general | solution.py:33
  26.3 0.0 all-reduce.4.cloned.1.call-update
  26.3 0.0 all-reduce.6.cloned.1.call-start
  26.4 9.3 %all_gather.7 = bf16[32,4,1024]{2,1,0:T(4,128)(2,1)S(1)} all-gather(bf16[4,4,1024]{2,1,0:T(4,128)(2,1)S(1)} %bitcast.60), channel_id=1, replica_groups=mesh['dp'=4,'tensor'=8] {'tensor'}, dimensions={0}, use_global_device_ids=true | all-gather | bytes 294912 | tf_op jit(solution)/shard_map/all_gather | solution.py:38
  35.7 0.2 multiply_reduce_fusion.2
  35.9 0.1 copy.41
  36.0 12.4 %psum.42 = f32[4,32]{1,0:T(4,128)S(1)} all-reduce(f32[4,32]{1,0:T(4,128)S(1)} %bitcast.62), channel_id=1, replica_groups=mesh['dp'=4,'tensor'=8] {'dp'}, use_global_device_ids=true, to_apply=%region_1.0 | all-reduce | flops 128 | bytes 1024 | tf_op jit(solution)/shard_map/psum | solution.py:39
  48.4 0.1 copy.33
  48.5 1.1 broadcast_multiply_fusion
  49.6 1.2 reshape.46
  50.8 0.0 slice-start.1
  50.8 5.3 %convolution_convert_fusion.4 = bf16[128,3584]{1,0:T(8,128)(2,1)} fusion(bf16[128,1024]{1,0:T(8,128)(2,1)S(1)} %reshape.46, bf16[1024,3584]{1,0:T(8,128)(2,1)} %param.9), kind=kOutput, calls=%fused_computation.4 | convolution fusion | flops 939982848 | bytes 8519680 | tf_op jit(solution)/shard_map/dot_general | solution.py:57
  56.1 2.1 convolution_convert_fusion.3
  58.2 16.7 %all-reduce.4.cloned.1.call-done = bf16[128,3584]{1,0:T(8,128)(2,1)} async-done(((bf16[128,3584]{1,0:T(8,128)(2,1)}), bf16[128,3584]{1,0:T(8,128)(2,1)}) %all-reduce.4.cloned.1.call-update) | async-done | bytes 917520 | tf_op jit(solution)/shard_map/psum | solution.py:36
  74.9 0.0 all-reduce.6.cloned.1.call-update
  74.9 0.2 reduce-scatter.2.cloned.1.call-start
  75.1 0.8 reshape.50
  75.9 1.0 reshape.49
  76.9 0.1 mul.126
  77.0 77.6 %all-reduce.6.cloned.1.call-done = (bf16[128,3584]{1,0:T(8,128)(2,1)}, bf16[128,3584]{1,0:T(8,128)(2,1)}) async-done(((bf16[128,3584]{1,0:T(8,128)(2,1)}, bf16[128,3584]{1,0:T(8,128)(2,1)}), (bf16[128,3584]{1,0:T(8,128)(2,1)}, bf16[128,3584]{1,0:T(8,128)(2,1)})) %all-reduce.6.cloned.1.call-update) | async-done | bytes 1835024 | tf_op jit(solution)/shard_map/psum | solution.py:61
  154.6 2.2 %fusion.1 = bf16[128,3584]{1,0:T(8,128)(2,1)S(1)} fusion(bf16[128,3584]{1,0:T(8,128)(2,1)} %get-tuple-element.35, f32[128]{0:T(128)S(1)} %mul.126, bf16[128,3584]{1,0:T(8,128)(2,1)} %get-tuple-element.36), kind=kLoop, calls=%fused_computation.13 | loop fusion | flops 4128768 | bytes 2753024 | tf_op jit(solution)/shard_map/convert_element_type | solution.py:15
  156.9 0.0 slice-start.3
  156.9 6.0 %fusion.25 = f32[128,1024]{1,0:T(8,128)S(1)} fusion(bf16[1024,3584]{1,0:T(8,128)(2,1)} %param.9, bf16[128,3584]{1,0:T(8,128)(2,1)S(1)} %copy-done.5, bf16[128,3584]{1,0:T(8,128)(2,1)} %all-reduce.4.cloned.1.call-done, bf16[128,3584]{1,0:T(8,128)(2,1)S(1)} %copy-done.6, f32[128]{0:T(128)S(1)} %mul.126), kind=kOutput, calls=%fused_computation.54 | convolution fusion | flops 945946624 | bytes 10617344 | tf_op jit(solution)/shard_map/dot_general | solution.py:72
  163.0 5.4 %convolution_convert_fusion.1 = bf16[1024,3584]{1,0:T(8,128)(2,1)} fusion(bf16[128,1024]{1,0:T(8,128)(2,1)S(1)} %reshape.46, bf16[128,3584]{1,0:T(8,128)(2,1)S(1)} %copy-done.13, f32[128]{0:T(128)S(1)} %mul.126, bf16[128,3584]{1,0:T(8,128)(2,1)S(1)} %copy-done.6), kind=kOutput, calls=%fused_computation.1 | convolution fusion | flops 947322880 | bytes 9437696 | tf_op jit(solution)/shard_map/dot_general | solution.py:110
  168.4 2.7 %multiply_reduce_fusion.1 = (f32[1024]{0:T(1024)S(1)}, f32[128]{0:T(128)S(1)}, bf16[128,1024]{1,0:T(8,128)(2,1)S(1)}) fusion(f32[128,1024]{1,0:T(8,128)S(1)} %copy-done.9, f32[128,1024]{1,0:T(8,128)S(1)} %copy-done.8, f32[1024]{0:T(1024)S(1)} %copy-done.12, f32[128,1024]{1,0:T(8,128)S(1)} %fusion.25, bf16[1024,3584]{1,0:T(8,128)(2,1)S(1)} %bitcast.57, ...), kind=kOutput, calls=%fused_computation.28 | convolution fusion | flops 944569216 | bytes 11019264 | tf_op jit(solution)/shard_map/dot_general | solution.py:74
  171.0 0.1 stack_reshape.9
  171.2 0.1 copy.35
  171.2 4.2 %convolution_convert_fusion.6 = bf16[128,1024]{1,0:T(8,128)(2,1)S(1)} fusion(bf16[128,3584]{1,0:T(8,128)(2,1)S(1)} %fusion.1, bf16[3584,1024]{1,0:T(8,128)(2,1)} %param.11), kind=kOutput, calls=%fused_computation.25 | convolution fusion | flops 939655168 | bytes 8519680 | tf_op jit(solution)/shard_map/dot_general | solution.py:71
  175.5 0.1 stack_reshape.8
  175.6 0.1 copy.34
  175.7 0.1 pad_maximum_fusion
  175.7 1.1 copy.36
  176.8 0.0 reduce-scatter.2.cloned.1.call-update
  176.8 5.1 %convolution_convert_fusion = bf16[3584,1024]{1,0:T(8,128)(2,1)} fusion(bf16[128,3584]{1,0:T(8,128)(2,1)S(1)} %fusion.1, bf16[128,1024]{1,0:T(8,128)(2,1)S(1)} %copy-done.3), kind=kOutput, calls=%fused_computation | convolution fusion | flops 943194112 | bytes 8519680 | tf_op jit(solution)/shard_map/dot_general | solution.py:104
  182.0 12.8 %psum.46 = f32[1152]{0:T(1024)S(1)} all-reduce(f32[1152]{0:T(1024)S(1)} %pad_maximum_fusion.1), channel_id=1, replica_groups=mesh['dp'=4,'tensor'=8] {'tensor'}, use_global_device_ids=true, to_apply=%region_8.0 | all-reduce | flops 1152 | bytes 9216 | tf_op jit(solution)/shard_map/psum | solution.py:93
  194.8 0.6 slice.19
  195.4 0.1 reshape.51
  195.5 0.1 copy.39
  195.6 11.1 %psum.47 = f32[32,4]{0,1:T(4,128)S(1)} all-reduce(f32[32,4]{0,1:T(4,128)S(1)} %copy.39), channel_id=1, replica_groups=mesh['dp'=4,'tensor'=8] {'dp'}, use_global_device_ids=true, to_apply=%region_9.0 | all-reduce | flops 128 | bytes 1024 | tf_op jit(solution)/shard_map/psum | solution.py:95
  206.7 0.7 fusion.20
  207.4 6.6 %convolution_convert_fusion.2 = bf16[1024,3584]{1,0:T(8,128)(2,1)} fusion(bf16[128,1024]{1,0:T(8,128)(2,1)S(1)} %reshape.46, bf16[128,3584]{1,0:T(8,128)(2,1)S(1)} %copy-done.5, bf16[128,3584]{1,0:T(8,128)(2,1)} %all-reduce.4.cloned.1.call-done, bf16[128,3584]{1,0:T(8,128)(2,1)S(1)} %copy-done.7, f32[128]{0:T(128)S(1)} %mul.126), kind=kOutput, calls=%fused_computation.2 | convolution fusion | flops 949616640 | bytes 10355200 | tf_op jit(solution)/shard_map/dot_general | solution.py:107
  214.0 0.9 copy.40
  214.9 0.7 fusion.14
  (44 shorter events, 0.1 us)
Async XLA Ops:
  7.2 67.7 %all-reduce.4.cloned.1.call-start = ((), (), s32[]{:S(2)}) async-start(), calls=%async_computation.1 | async-start | bytes 1835008 | tf_op jit(solution)/shard_map/psum | solution.py:36
  19.6 6.7 %copy-start.2 = (bf16[128,1024]{1,0:T(8,128)(2,1)}, bf16[128,1024]{1,0:T(8,128)(2,1)S(1)}, u32[]{:S(2)}) copy-start(bf16[128,1024]{1,0:T(8,128)(2,1)S(1)} %reshape.45) | copy-start | bytes 786436
  19.6 28.9 %copy-start.12 = (f32[1024]{0:T(1024)S(1)}, f32[1024]{0:T(1024)}, u32[]{:S(2)}) copy-start(f32[1024]{0:T(1024)} %param.8) | copy-start | bytes 12292
  26.3 128.3 %all-reduce.6.cloned.1.call-start = ((), (), s32[]{:S(2)}) async-start(), calls=%async_computation.3 | async-start | bytes 3670016 | tf_op jit(solution)/shard_map/psum | solution.py:61
  35.7 13.9 %copy-start = (bf16[32,4,1024]{2,1,0:T(4,128)(2,1)}, bf16[32,4,1024]{2,1,0:T(4,128)(2,1)S(1)}, u32[]{:S(2)}) copy-start(bf16[32,4,1024]{2,1,0:T(4,128)(2,1)S(1)} %all_gather.7) | copy-start | bytes 786436
  49.6 6.5 %slice-start = ((s8[7340032]{0:T(1024)(128)(4,1)}), s8[3145728]{0:T(1024)(128)(4,1)S(1)}, s32[]{:S(2)}) async-start(s8[7340032]{0:T(1024)(128)(4,1)} %bitcast.54), calls=%async_computation.4 | async-start | bytes 6291456
  50.8 5.3 %slice-start.1 = ((s8[7340032]{0:T(1024)(128)(4,1)}), s8[4194304]{0:T(1024)(128)(4,1)S(1)}, s32[]{:S(2)}) async-start(s8[7340032]{0:T(1024)(128)(4,1)} %bitcast.54), calls=%async_computation.5 | async-start | bytes 8388608
  58.2 17.0 %copy-start.1 = (bf16[32,4,1024]{2,1,0:T(4,128)(2,1)S(1)}, bf16[32,4,1024]{2,1,0:T(4,128)(2,1)}, u32[]{:S(2)}) copy-start(bf16[32,4,1024]{2,1,0:T(4,128)(2,1)} %copy-done) | copy-start | bytes 786436
  58.2 17.8 %copy-start.4 = (f32[32,4,1024]{2,1,0:T(4,128)S(1)}, f32[32,4,1024]{2,1,0:T(4,128)}, u32[]{:S(2)}) copy-start(f32[32,4,1024]{2,1,0:T(4,128)} %get-tuple-element.41) | copy-start | bytes 1572868
  58.2 18.8 %copy-start.14 = (s32[4]{0:T(128)S(1)}, s32[4]{0:T(128)}, u32[]{:S(2)}) copy-start(s32[4]{0:T(128)} %param.13) | copy-start | bytes 52
  74.9 139.1 %reduce-scatter.2.cloned.1.call-start = ((), (), s32[]{:S(2)}) async-start(), calls=%async_computation.2 | async-start | bytes 589824 | tf_op jit(solution)/shard_map/reduce_scatter | solution.py:98
  154.6 2.3 %copy-start.5 = (bf16[128,3584]{1,0:T(8,128)(2,1)S(1)}, bf16[128,3584]{1,0:T(8,128)(2,1)}, u32[]{:S(2)}) copy-start(bf16[128,3584]{1,0:T(8,128)(2,1)} %get-tuple-element.35) | copy-start | bytes 2752516
  154.6 2.3 %copy-start.6 = (bf16[128,3584]{1,0:T(8,128)(2,1)S(1)}, bf16[128,3584]{1,0:T(8,128)(2,1)}, u32[]{:S(2)}) copy-start(bf16[128,3584]{1,0:T(8,128)(2,1)} %get-tuple-element.36) | copy-start | bytes 2752516
  154.6 13.7 %slice-start.2 = ((s8[7340032]{0:T(1024)(128)(4,1)}), s8[4194304]{0:T(1024)(128)(4,1)S(1)}, s32[]{:S(2)}) async-start(s8[7340032]{0:T(1024)(128)(4,1)} %bitcast.56), calls=%async_computation.6 | async-start | bytes 8388608
  156.9 6.1 %copy-start.13 = (bf16[128,3584]{1,0:T(8,128)(2,1)S(1)}, bf16[128,3584]{1,0:T(8,128)(2,1)}, u32[]{:S(2)}) copy-start(bf16[128,3584]{1,0:T(8,128)(2,1)} %all-reduce.4.cloned.1.call-done) | copy-start | bytes 2752516
  156.9 11.5 %slice-start.3 = ((s8[7340032]{0:T(1024)(128)(4,1)}), s8[3145728]{0:T(1024)(128)(4,1)S(1)}, s32[]{:S(2)}) async-start(s8[7340032]{0:T(1024)(128)(4,1)} %bitcast.56), calls=%async_computation.7 | async-start | bytes 6291456
  162.9 5.4 %copy-start.8 = (f32[128,1024]{1,0:T(8,128)S(1)}, f32[128,1024]{1,0:T(8,128)}, u32[]{:S(2)}) copy-start(f32[128,1024]{1,0:T(8,128)} %reshape.50) | copy-start | bytes 1572868
  163.0 5.4 %copy-start.9 = (f32[128,1024]{1,0:T(8,128)S(1)}, f32[128,1024]{1,0:T(8,128)}, u32[]{:S(2)}) copy-start(f32[128,1024]{1,0:T(8,128)} %reshape.49) | copy-start | bytes 1572868
  175.5 1.4 copy-start.3
  176.8 30.5 %copy-start.7 = (bf16[128,3584]{1,0:T(8,128)(2,1)S(1)}, bf16[128,3584]{1,0:T(8,128)(2,1)}, u32[]{:S(2)}) copy-start(bf16[128,3584]{1,0:T(8,128)(2,1)} %get-tuple-element.36) | copy-start | bytes 2752516
  207.4 7.5 %copy-start.10 = (bf16[4,4,1024]{2,1,0:T(4,128)(2,1)S(1)}, bf16[4,4,1024]{2,1,0:T(4,128)(2,1)}, u32[]{:S(2)}) copy-start(bf16[4,4,1024]{2,1,0:T(4,128)(2,1)} %param.7) | copy-start | bytes 98308
  207.4 7.5 %copy-start.11 = (bf16[4,4,1024]{2,1,0:T(4,128)(2,1)S(1)}, bf16[4,4,1024]{2,1,0:T(4,128)(2,1)}, u32[]{:S(2)}) copy-start(bf16[4,4,1024]{2,1,0:T(4,128)(2,1)} %param.12) | copy-start | bytes 98308
Sparse Core Ops, SparseCore 0:
  26.4 48.3 all-reduce.3
  77.8 76.7 all-reduce.5
  176.9 33.0 reduce-scatter.1
where the time goes:
time: 223 us; the launch traced here: 222 us
  waiting for transfers between devices  94.3 us (42%)
  blocking collectives  56.5 us (25%)
  matrix products  44 us (20%)
  between operations  14 us (6%)
  local copies, waits for them, and re-layouts  8.07 us (4%)
  other arithmetic  4.98 us (2%)
    psum x1, waiting for transfers between devices, per_device(): gate_sum, up_sum = lax.psum(parts, 'dp')  77.6 us
    psum x1, waiting for transfers between devices, per_device(): back_first = lax.psum(back_part, 'dp')  16.7 us
    psum x1, blocking collectives, per_device(): reduced = lax.psum(jnp.concatenate([gain_part, row_all]), 'tensor')  12.8 us
    psum x1, blocking collectives, per_device(): square_sum = lax.psum(jnp.sum(inputs_all * inputs_all, axis=2).T, 'dp').T  12.4 us
    psum x1, blocking collectives, per_device(): row_all = lax.psum(reduced[local_feat:], 'dp').reshape(rows, batches)  11.1 us
    all_gather x1, blocking collectives, per_device(): lax.all_gather(d_output.transpose(1, 0, 2), 'tensor', axis=0, tiled=True)  10.8 us
    all_gather x1, blocking collectives, per_device(): lax.all_gather(inputs_all, 'tensor', axis=0, tiled=True).astype(jnp.float32)  9.28 us
    dot_general x1, matrix products, per_device(): lax.dot_general(flat_grad, w_down, contract_cols, preferred_element_type=...  6.65 us
  transfers between devices with their start and end apart: 3, of which 2 were waited for; matrix products, arithmetic and copies ran while one was open for 11% of the time, Pallas kernels for 0%

commit v1 on v0

--- a/solution.py
+++ b/solution.py
@@ -33,7 +33,11 @@
     back_part = lax.dot_general(
         flat_grad, w_down, contract_cols, preferred_element_type=jnp.float32
     ).astype(jnp.bfloat16)
-    back_first = lax.psum(back_part, "dp")
+    back_first = back_part
+    for hop in (1, 2):
+        back_first = back_first + lax.ppermute(
+            back_first, "dp", [(dev, dev ^ hop) for dev in range(4)]
+        )
     inputs_all, _ = lax.optimization_barrier((inputs.transpose(1, 0, 2), back_part))
     inputs_all = lax.all_gather(inputs_all, "tensor", axis=0, tiled=True).astype(jnp.float32)
     square_sum = lax.psum(jnp.sum(inputs_all * inputs_all, axis=2).T, "dp").T

time: 223 us -> 242 us (1.085)
  waiting for transfers between devices: 94.3 us -> 108 us
  blocking collectives: 56.5 us -> 60.9 us
    ppermute x0 -> x2, waiting for transfers between devices: none -> 33.5 us  [per_device(): lax.ppermute(back_first, 'dp', [(dev, dev ^ hop) for dev in range(4)])]
    psum x1 -> x0, waiting for transfers between devices: 16.7 us -> none  [per_device(): back_first = lax.psum(back_part, 'dp')]
    psum x1, blocking collectives: 12.4 us -> 16.9 us  [per_device(): square_sum = lax.psum(jnp.sum(inputs_all * inputs_all, axis=2).T, 'dp').T]
    psum x1, waiting for transfers between devices: 77.6 us -> 74.8 us  [per_device(): gate_sum, up_sum = lax.psum(parts, 'dp')]
    add x0 -> x2, other arithmetic: none -> 2.69 us  [per_device(): back_first + lax.ppermute(back_first, 'dp', [(dev, dev ^ hop) for dev in...]
  transfers between devices with their start and end apart: 3 -> 4, of which waited for: 2 -> 2; matrix products, arithmetic and copies ran while one was open for 11% -> 9% of each run, Pallas kernels for 0% -> 0%
where the time goes in v1:
time: 242 us; the launch traced here: 241 us
  waiting for transfers between devices  108 us (45%)
  blocking collectives  60.9 us (25%)
  matrix products  43.4 us (18%)
  between operations  14.3 us (6%)
  other arithmetic  6.79 us (3%)
  local copies, waits for them, and re-layouts  5.72 us (2%)
    psum x1, waiting for transfers between devices, per_device(): gate_sum, up_sum = lax.psum(parts, 'dp')  74.8 us
    ppermute x2, waiting for transfers between devices, per_device(): lax.ppermute(back_first, 'dp', [(dev, dev ^ hop) for dev in range(4)])  33.5 us
    psum x1, blocking collectives, per_device(): square_sum = lax.psum(jnp.sum(inputs_all * inputs_all, axis=2).T, 'dp').T  16.9 us
    psum x1, blocking collectives, per_device(): reduced = lax.psum(jnp.concatenate([gain_part, row_all]), 'tensor')  12.8 us
    psum x1, blocking collectives, per_device(): row_all = lax.psum(reduced[local_feat:], 'dp').reshape(rows, batches)  11.2 us
    all_gather x1, blocking collectives, per_device(): lax.all_gather(d_output.transpose(1, 0, 2), 'tensor', axis=0, tiled=True)  10.8 us
    all_gather x1, blocking collectives, per_device(): lax.all_gather(inputs_all, 'tensor', axis=0, tiled=True).astype(jnp.float32)  9.28 us
    dot_general x1, matrix products, per_device(): lax.dot_general(flat_normed, gate_grad, contract_rows, preferred_element_...  6.6 us
  transfers between devices with their start and end apart: 4, of which 2 were waited for; matrix products, arithmetic and copies ran while one was open for 9% of the time, Pallas kernels for 0%

profile of v1, /device:TPU:0, one launch (start us, length us, event | category | flops | bytes accessed | tf_op | source)
XLA Modules:
  0.0 241.4 jit_solution(16646918865670711454)
XLA Ops:
  7.2 0.0 all-reduce.3.cloned.1.call-start
  7.2 0.8 copy.44
  8.0 10.8 %all_gather.6 = bf16[32,4,1024]{2,1,0:T(4,128)(2,1)S(1)} all-gather(bf16[4,4,1024]{2,1,0:T(4,128)(2,1)S(1)} %bitcast.60), channel_id=1, replica_groups=mesh['dp'=4,'tensor'=8] {'tensor'}, dimensions={0}, use_global_device_ids=true | all-gather | bytes 294912 | tf_op jit(solution)/shard_map/all_gather | solution.py:29
  18.8 0.1 reshape.45
  18.9 5.6 %convolution_convert_fusion.5 = bf16[128,3584]{1,0:T(8,128)(2,1)S(1)} fusion(bf16[128,1024]{1,0:T(8,128)(2,1)S(1)} %reshape.45, bf16[3584,1024]{1,0:T(8,128)(2,1)} %param.11), kind=kOutput, calls=%fused_computation.5 | convolution fusion | flops 939982848 | bytes 8519680 | tf_op jit(solution)/shard_map/dot_general | solution.py:33
  24.5 1.6 collective-permute-start
  26.2 9.3 %all_gather.7 = bf16[32,4,1024]{2,1,0:T(4,128)(2,1)S(1)} all-gather(bf16[4,4,1024]{2,1,0:T(4,128)(2,1)S(1)} %bitcast.61), channel_id=1, replica_groups=mesh['dp'=4,'tensor'=8] {'tensor'}, dimensions={0}, use_global_device_ids=true | all-gather | bytes 294912 | tf_op jit(solution)/shard_map/all_gather | solution.py:42
  35.4 0.2 multiply_reduce_fusion.2
  35.7 0.1 copy.41
  35.7 16.9 %psum.35 = f32[4,32]{1,0:T(4,128)S(1)} all-reduce(f32[4,32]{1,0:T(4,128)S(1)} %bitcast.62), channel_id=1, replica_groups=mesh['dp'=4,'tensor'=8] {'dp'}, use_global_device_ids=true, to_apply=%region_1.0 | all-reduce | flops 128 | bytes 1024 | tf_op jit(solution)/shard_map/psum | solution.py:43
  52.6 0.1 copy.33
  52.7 0.2 broadcast_multiply_fusion
  52.9 0.1 reshape.46
  53.0 1.5 add.46
  54.6 0.0 slice-start.1
  54.6 0.1 collective-permute-start.1
  54.7 5.3 %convolution_convert_fusion.4 = bf16[128,3584]{1,0:T(8,128)(2,1)} fusion(bf16[128,1024]{1,0:T(8,128)(2,1)S(1)} %reshape.46, bf16[1024,3584]{1,0:T(8,128)(2,1)} %param.9), kind=kOutput, calls=%fused_computation.4 | convolution fusion | flops 939982848 | bytes 8519680 | tf_op jit(solution)/shard_map/dot_general | solution.py:61
  60.0 2.1 convolution_convert_fusion.3
  62.0 33.5 %collective-permute-done.1 = bf16[128,3584]{1,0:T(8,128)(2,1)S(1)} collective-permute-done((bf16[128,3584]{1,0:T(8,128)(2,1)S(1)}, bf16[128,3584]{1,0:T(8,128)(2,1)S(1)}, u32[]{:S(2)}, u32[]{:S(2)}) %collective-permute-start.1) | collective-permute-done | bytes 917536 | tf_op jit(solution)/shard_map/ppermute | solution.py:38
  95.5 1.2 add.47
  96.7 0.0 all-reduce.3.cloned.1.call-update
  96.7 0.2 reduce-scatter.2.cloned.1.call-start
  97.0 0.2 reshape.49
  97.2 0.1 copy-done.8
  97.3 0.1 mul.126
  97.4 74.8 %all-reduce.3.cloned.1.call-done = (bf16[128,3584]{1,0:T(8,128)(2,1)}, bf16[128,3584]{1,0:T(8,128)(2,1)}) async-done(((bf16[128,3584]{1,0:T(8,128)(2,1)}, bf16[128,3584]{1,0:T(8,128)(2,1)}), (bf16[128,3584]{1,0:T(8,128)(2,1)}, bf16[128,3584]{1,0:T(8,128)(2,1)})) %all-reduce.3.cloned.1.call-update) | async-done | bytes 1835024 | tf_op jit(solution)/shard_map/psum | solution.py:65
  172.2 2.2 fusion.1
  174.5 5.8 %fusion.25 = f32[128,1024]{1,0:T(8,128)S(1)} fusion(bf16[1024,3584]{1,0:T(8,128)(2,1)} %param.9, bf16[128,3584]{1,0:T(8,128)(2,1)S(1)} %copy-done, bf16[128,3584]{1,0:T(8,128)(2,1)S(1)} %copy-done.4, bf16[128,3584]{1,0:T(8,128)(2,1)S(1)} %copy-done.2, f32[128]{0:T(128)S(1)} %mul.126), kind=kOutput, calls=%fused_computation.54 | convolution fusion | flops 945946624 | bytes 10617344 | tf_op jit(solution)/shard_map/dot_general | solution.py:76
  180.3 5.4 %convolution_convert_fusion.1 = bf16[1024,3584]{1,0:T(8,128)(2,1)} fusion(bf16[128,1024]{1,0:T(8,128)(2,1)S(1)} %reshape.46, bf16[128,3584]{1,0:T(8,128)(2,1)S(1)} %copy-done.4, f32[128]{0:T(128)S(1)} %mul.126, bf16[128,3584]{1,0:T(8,128)(2,1)S(1)} %copy-done.2), kind=kOutput, calls=%fused_computation.1 | convolution fusion | flops 947322880 | bytes 9437696 | tf_op jit(solution)/shard_map/dot_general | solution.py:114
  185.7 3.3 %multiply_reduce_fusion.1 = (f32[1024]{0:T(1024)S(1)}, f32[128]{0:T(128)S(1)}, bf16[128,1024]{1,0:T(8,128)(2,1)}) fusion(f32[128,1024]{1,0:T(8,128)S(1)} %reshape.49, f32[128,1024]{1,0:T(8,128)S(1)} %reshape.50, f32[1024]{0:T(1024)S(1)} %copy-done.7, f32[128,1024]{1,0:T(8,128)S(1)} %fusion.25, bf16[1024,3584]{1,0:T(8,128)(2,1)S(1)} %bitcast.57, ...), kind=kOutput, calls=%fused_computation.28 | convolution fusion | flops 944569216 | bytes 11019264 | tf_op jit(solution)/shard_map/dot_general | solution.py:78
  189.0 1.1 stack_reshape.9
  190.0 0.1 copy.35
  190.1 4.2 %convolution_convert_fusion.6 = bf16[128,1024]{1,0:T(8,128)(2,1)S(1)} fusion(bf16[128,3584]{1,0:T(8,128)(2,1)S(1)} %fusion.1, bf16[3584,1024]{1,0:T(8,128)(2,1)} %param.11), kind=kOutput, calls=%fused_computation.25 | convolution fusion | flops 939655168 | bytes 8519680 | tf_op jit(solution)/shard_map/dot_general | solution.py:75
  194.3 0.1 stack_reshape.8
  194.5 0.1 copy.34
  194.5 0.1 pad_maximum_fusion
  194.6 1.1 copy.36
  195.7 0.0 reduce-scatter.2.cloned.1.call-update
  195.7 5.1 %convolution_convert_fusion = bf16[3584,1024]{1,0:T(8,128)(2,1)} fusion(bf16[128,3584]{1,0:T(8,128)(2,1)S(1)} %fusion.1, bf16[128,1024]{1,0:T(8,128)(2,1)S(1)} %reshape.45), kind=kOutput, calls=%fused_computation | convolution fusion | flops 943194112 | bytes 8519680 | tf_op jit(solution)/shard_map/dot_general | solution.py:108
  200.9 12.8 %psum.38 = f32[1152]{0:T(1024)S(1)} all-reduce(f32[1152]{0:T(1024)S(1)} %pad_maximum_fusion.1), channel_id=1, replica_groups=mesh['dp'=4,'tensor'=8] {'tensor'}, use_global_device_ids=true, to_apply=%region_7.0 | all-reduce | flops 1152 | bytes 9216 | tf_op jit(solution)/shard_map/psum | solution.py:97
  213.7 0.6 slice.19
  214.3 0.1 reshape.51
  214.4 0.1 copy.39
  214.5 11.2 %psum.39 = f32[32,4]{0,1:T(4,128)S(1)} all-reduce(f32[32,4]{0,1:T(4,128)S(1)} %copy.39), channel_id=1, replica_groups=mesh['dp'=4,'tensor'=8] {'dp'}, use_global_device_ids=true, to_apply=%region_8.0 | all-reduce | flops 128 | bytes 1024 | tf_op jit(solution)/shard_map/psum | solution.py:99
  225.7 0.7 fusion.20
  226.3 6.6 %convolution_convert_fusion.2 = bf16[1024,3584]{1,0:T(8,128)(2,1)} fusion(bf16[128,1024]{1,0:T(8,128)(2,1)S(1)} %reshape.46, bf16[128,3584]{1,0:T(8,128)(2,1)S(1)} %copy-done.1, bf16[128,3584]{1,0:T(8,128)(2,1)} %add.47, bf16[128,3584]{1,0:T(8,128)(2,1)S(1)} %copy-done.3, f32[128]{0:T(128)S(1)} %mul.126), kind=kOutput, calls=%fused_computation.2 | convolution fusion | flops 949616640 | bytes 10355200 | tf_op jit(solution)/shard_map/dot_general | solution.py:111
  232.9 0.9 copy.40
  233.8 0.7 fusion.14
  (35 shorter events, 0.1 us)
Async XLA Ops:
  7.2 165.1 %all-reduce.3.cloned.1.call-start = ((), (), s32[]{:S(2)}) async-start(), calls=%async_computation.2 | async-start | bytes 3670016 | tf_op jit(solution)/shard_map/psum | solution.py:65
  18.8 7.3 %copy-start.5 = (bf16[4,4,1024]{2,1,0:T(4,128)(2,1)S(1)}, bf16[4,4,1024]{2,1,0:T(4,128)(2,1)}, u32[]{:S(2)}) copy-start(bf16[4,4,1024]{2,1,0:T(4,128)(2,1)} %param.7) | copy-start | bytes 98308
  18.9 33.8 %copy-start.7 = (f32[1024]{0:T(1024)S(1)}, f32[1024]{0:T(1024)}, u32[]{:S(2)}) copy-start(f32[1024]{0:T(1024)} %param.8) | copy-start | bytes 12292
  24.5 28.5 %collective-permute-start = (bf16[128,3584]{1,0:T(8,128)(2,1)S(1)}, bf16[128,3584]{1,0:T(8,128)(2,1)}, u32[]{:S(2)}, u32[]{:S(2)}) collective-permute-start(bf16[128,3584]{1,0:T(8,128)(2,1)S(1)} %convolution_convert_fusion.5), channel_id=1, source_target_pairs={{0,8},{8,0},{16,24},{24,16},{1,9},{9,1},{17,25},{25,17},{2,10},{10... | collective-permute-start | bytes 2752520 | tf_op jit(solution)/shard_map/ppermute | solution.py:38
  53.0 6.9 %slice-start = ((s8[7340032]{0:T(1024)(128)(4,1)}), s8[4194304]{0:T(1024)(128)(4,1)S(1)}, s32[]{:S(2)}) async-start(s8[7340032]{0:T(1024)(128)(4,1)} %bitcast.54), calls=%async_computation.3 | async-start | bytes 8388608
  54.6 5.4 %slice-start.1 = ((s8[7340032]{0:T(1024)(128)(4,1)}), s8[3145728]{0:T(1024)(128)(4,1)S(1)}, s32[]{:S(2)}) async-start(s8[7340032]{0:T(1024)(128)(4,1)} %bitcast.54), calls=%async_computation.4 | async-start | bytes 6291456
  54.6 40.9 %collective-permute-start.1 = (bf16[128,3584]{1,0:T(8,128)(2,1)S(1)}, bf16[128,3584]{1,0:T(8,128)(2,1)S(1)}, u32[]{:S(2)}, u32[]{:S(2)}) collective-permute-start(bf16[128,3584]{1,0:T(8,128)(2,1)S(1)} %add.46), channel_id=1, source_target_pairs={{0,16},{8,24},{16,0},{24,8},{1,17},{9,25},{17,1},{25,9},{2,18},{10... | collective-permute-start | bytes 2752520 | tf_op jit(solution)/shard_map/ppermute | solution.py:38
  96.7 0.7 copy-start.8
  96.7 136.2 %reduce-scatter.2.cloned.1.call-start = ((), (), s32[]{:S(2)}) async-start(), calls=%async_computation.1 | async-start | bytes 589824 | tf_op jit(solution)/shard_map/reduce_scatter | solution.py:102
  97.0 77.5 %copy-start.4 = (bf16[128,3584]{1,0:T(8,128)(2,1)S(1)}, bf16[128,3584]{1,0:T(8,128)(2,1)}, u32[]{:S(2)}) copy-start(bf16[128,3584]{1,0:T(8,128)(2,1)} %add.47) | copy-start | bytes 2752516
  172.2 2.3 copy-start
  172.2 2.3 copy-start.2
  172.2 13.5 %slice-start.2 = ((s8[7340032]{0:T(1024)(128)(4,1)}), s8[4194304]{0:T(1024)(128)(4,1)S(1)}, s32[]{:S(2)}) async-start(s8[7340032]{0:T(1024)(128)(4,1)} %bitcast.56), calls=%async_computation.5 | async-start | bytes 8388608
  174.5 11.2 %slice-start.3 = ((s8[7340032]{0:T(1024)(128)(4,1)}), s8[3145728]{0:T(1024)(128)(4,1)S(1)}, s32[]{:S(2)}) async-start(s8[7340032]{0:T(1024)(128)(4,1)} %bitcast.56), calls=%async_computation.6 | async-start | bytes 6291456
  195.7 30.6 %copy-start.1 = (bf16[128,3584]{1,0:T(8,128)(2,1)S(1)}, bf16[128,3584]{1,0:T(8,128)(2,1)}, u32[]{:S(2)}) copy-start(bf16[128,3584]{1,0:T(8,128)(2,1)} %get-tuple-element.35) | copy-start | bytes 2752516
  195.7 30.6 %copy-start.3 = (bf16[128,3584]{1,0:T(8,128)(2,1)S(1)}, bf16[128,3584]{1,0:T(8,128)(2,1)}, u32[]{:S(2)}) copy-start(bf16[128,3584]{1,0:T(8,128)(2,1)} %get-tuple-element.36) | copy-start | bytes 2752516
  226.3 7.5 %copy-start.6 = (bf16[4,4,1024]{2,1,0:T(4,128)(2,1)S(1)}, bf16[4,4,1024]{2,1,0:T(4,128)(2,1)}, u32[]{:S(2)}) copy-start(bf16[4,4,1024]{2,1,0:T(4,128)(2,1)} %param.12) | copy-start | bytes 98308
Sparse Core Ops, SparseCore 0:
  96.8 75.3 all-reduce.2
  195.8 33.1 reduce-scatter.1
